TPU v7x, 32 devices: a whole 2x2x4 slice. The times are simulated.
32 devices in a mesh: grp: 4 (over x, core), rel: 8 (over z, y).
Axes of the slice: x: 2, y: 2, z: 4, core: 2. Of those that a mesh axis runs over, the one named last changes fastest.
Arguments:
- head_ids: int32 [65536], P(('grp', 'rel')), may hold values from 0 to 1023
- relations: int32 [65536, 1], P(('grp', 'rel')), may hold values from 0 to 31; in each aligned block of 2048 rows (0 to 2047, 2048 to 4095, ...) at most 128 rows name the same one
- tail_ids: int32 [65536], P(('grp', 'rel')), may hold values from 0 to 1023
- neg_owner: int32 [1], replicated, may hold values from 0 to 31
- entities: bfloat16 [32768, 512], P(('grp', 'rel')), may hold values from -0.3984375 to 0.3984375
- rel_weight: float32 [32, 512, 512], P('rel'), may hold values from -6 to 6
- rel_accum: float32 [32, 512], P('rel'), may hold values from 0.001 to 0.1
Outputs:
- losses: bfloat16 [65536], P(('grp', 'rel'))
- head_grad: bfloat16 [65536, 512], P(('grp', 'rel'))
- new_rel: float32 [32, 512, 512], P('rel')
- new_accum: float32 [32, 512], P('rel')
Inputs may be any that keep to these rules, and one draw needn't show every extreme that they name: `head_ids`: a row of the device's own shard of 1024 entity rows. `tail_ids`: a row of the device's own shard of 1024 entity rows. `relations`: in the 2048 rows of one device no relation is named by more than 128 rows; some relation is named by exactly 128. `neg_owner`: a device index, counted grp first, then rel.
All inputs are finite; a program needn't handle non-finite values.
Results may differ from a plain program's by a relative error of at most 0.0095.
Values may be sent and summed in bfloat16 or wider, within the bound.
No kernel may reach another device: no remote copies, remote signals or barrier semaphores. Data moves between devices by JAX's collectives and lax.ppermute only.
A program may use at most 128 MiB of HBM per device.

v0:
```python
import jax
import jax.numpy as jnp
from jax import lax
from jax.sharding import PartitionSpec as P

LEARNING_RATE = 1.0


def broadcast(shard, axis, root):
    mine = lax.axis_index(axis) == root
    return lax.psum(jnp.where(mine, shard, jnp.zeros_like(shard)), axis)


def slot_ranks(rel_ids, bucket_count):
    one_hot = (rel_ids[..., None] == jnp.arange(bucket_count, dtype=jnp.int32)).astype(jnp.int32)
    running = jnp.cumsum(one_hot, axis=-2) - 1
    return jnp.sum(one_hot * running, axis=-1)


def score_rows(query_rows, tail_rows, negatives):
    positive = jnp.sum(query_rows.astype(jnp.float32) * tail_rows.astype(jnp.float32), axis=-1)
    neg_scores = jnp.dot(query_rows, negatives.T, preferred_element_type=jnp.float32)
    losses = jax.nn.softplus(-positive) + jnp.mean(jax.nn.softplus(neg_scores), axis=-1)
    coefs = (jax.nn.sigmoid(neg_scores) / negatives.shape[0]).astype(jnp.bfloat16)
    grad_query = -jax.nn.sigmoid(-positive)[:, None] * tail_rows.astype(jnp.float32)
    grad_query = grad_query + jnp.dot(coefs, negatives, preferred_element_type=jnp.float32)
    return (losses.astype(jnp.bfloat16), grad_query.astype(jnp.bfloat16))


def adagrad(weight, accumulator, gradient):
    new_accum = accumulator + jnp.mean(gradient * gradient, axis=-1)
    return (weight - LEARNING_RATE * gradient / jnp.sqrt(new_accum)[..., None], new_accum)


def to_buckets(values, position, layout):
    flat_shape = (layout[0] * layout[1] * layout[2],) + values.shape[1:]
    filled = jnp.zeros(flat_shape, values.dtype).at[position].set(values)
    return filled.reshape(layout + values.shape[1:])


def from_buckets(stacked, position):
    return stacked.reshape((-1,) + stacked.shape[3:])[position]


def per_device(head_ids, relations, tail_ids, neg_owner, entities, rel_weight, rel_accum):
    rows_here = head_ids.shape[0]
    width = entities.shape[1]
    owner_count = lax.axis_size("rel")
    local_rels = rel_weight.shape[0]
    capacity = 2 * rows_here // (owner_count * local_rels)
    layout = (owner_count, local_rels, capacity)
    rel_ids = relations[:, 0]
    position = rel_ids * capacity + slot_ranks(rel_ids, owner_count * local_rels)
    head_rows = jnp.take(entities, head_ids, axis=0)
    tail_rows = jnp.take(entities, tail_ids, axis=0)
    matrices = rel_weight.astype(jnp.bfloat16)
    negatives = broadcast(entities, ("grp", "rel"), neg_owner[0])
    held_rows, held_tails = (
        lax.all_to_all(
            to_buckets(head_rows, position, layout), "rel", split_axis=0, concat_axis=0, tiled=True
        ),
        lax.all_to_all(
            to_buckets(tail_rows, position, layout), "rel", split_axis=0, concat_axis=0, tiled=True
        ),
    )
    projected = jnp.einsum(
        "srcd,rde->srce", held_rows, matrices, preferred_element_type=jnp.float32
    ).astype(jnp.bfloat16)
    slot_losses, slot_grads = score_rows(
        projected.reshape(-1, width), held_tails.reshape(-1, width), negatives
    )
    grad_rows = slot_grads.reshape(held_rows.shape)
    partial_value = jnp.einsum(
        "srcd,srce->rde", held_rows, grad_rows, preferred_element_type=jnp.float32
    )
    head_back = jnp.einsum(
        "srce,rde->srcd", grad_rows, matrices, preferred_element_type=jnp.float32
    ).astype(jnp.bfloat16)
    partial_value, head_back = (partial_value, head_back)
    back_grads, back_losses = (
        lax.all_to_all(head_back, "rel", split_axis=0, concat_axis=0, tiled=True),
        lax.all_to_all(slot_losses.reshape(layout), "rel", split_axis=0, concat_axis=0, tiled=True),
    )
    head_grad = from_buckets(back_grads, position)
    losses = from_buckets(back_losses, position)
    summed = lax.psum(partial_value.astype(jnp.bfloat16), "grp").astype(jnp.float32)
    new_rel, new_accum = adagrad(rel_weight, rel_accum, summed)
    return (losses, head_grad, new_rel, new_accum)


def solution(mesh):
    placed = (
        P(("grp", "rel")),
        P(("grp", "rel"), None),
        P(("grp", "rel")),
        P(),
        P(("grp", "rel"), None),
        P("rel", None, None),
        P("rel", None),
    )
    return jax.shard_map(
        per_device,
        mesh=mesh,
        in_specs=placed,
        out_specs=(
            P(("grp", "rel")),
            P(("grp", "rel"), None),
            P("rel", None, None),
            P("rel", None),
        ),
        check_vma=False,
    )
```

profile of v0, /device:TPU:0, one launch (start us, length us, event | category | flops | bytes accessed | tf_op | source)
XLA Modules:
  0.0 504.7 jit_solution(10861121189316165478)
XLA Ops:
  7.2 0.7 compare_and_fusion
  7.9 0.7 fusion.34
  8.6 0.7 fusion.30
  9.3 9.1 %reduce-window.6 = s32[32,16,128]{2,1,0:T(8,128)S(1)} reduce-window(s32[32,16,128]{2,1,0:T(8,128)S(1)} %fusion.30, s32[]{:T(128)} %constant.22.clone.1), window={size=1x1x128 pad=0_0x0_0x127_0}, to_apply=%region_0.0 | reduce-window | flops 8323072 | bytes 524292 | tf_op jit(solution)/shard_map/reduce-window
  18.4 0.1 slice.16
  18.5 0.2 copy.60
  18.7 0.2 reduce-window.9
  18.9 0.1 add_add_fusion
  19.1 0.8 fusion.29
  19.9 0.7 compare_select_fusion.1
  20.6 27.7 %scatter_custom_fusion.1 = bf16[4096,512]{1,0:T(8,128)(2,1)} fusion(s32[2048]{0:T(1024)S(1)} %bitcast.69, bf16[]{:T(256)} %constant.20.clone.1, pred[2048]{0:T(1024)(128)(4,1)S(1)} %compare_and_fusion, bf16[]{:T(256)} %constant.15.clone.2, bf16[1024,512]{1,0:T(8,128)(2,1)} %param.13, s32[2048]{0:T(1024)S(1)} %fusion.34), kind=kCustom, calls=%fused_computation.28 | custom fusion | flops 1048576 | bytes 5253124 | tf_op jit(solution)/shard_map/scatter | solution.py:37
  48.3 0.0 copy-start.2
  48.3 0.0 copy-start
  48.3 7.4 %all-to-all-start.1 = ((bf16[8,4,128,512]{3,2,1,0:T(8,128)(2,1)}), bf16[8,4,128,512]{3,2,1,0:T(8,128)(2,1)}, u32[]{:S(2)}, u32[]{:S(2)}) async-start(bf16[8,4,128,512]{3,2,1,0:T(8,128)(2,1)} %bitcast.60), calls=%async_computation.1 | async-start | bytes 8388608 | tf_op jit(solution)/shard_map/all_to_all | solution.py:62
  55.7 0.0 copy-done.2
  55.8 0.0 copy-done
  55.8 22.6 %scatter_custom_fusion = bf16[4096,512]{1,0:T(8,128)(2,1)} fusion(s32[2048]{0:T(1024)S(1)} %bitcast.70, bf16[]{:T(256)} %constant.20.clone.1, pred[2048]{0:T(1024)(128)(4,1)S(1)} %compare_and_fusion.1, bf16[]{:T(256)} %constant.15.clone.2, bf16[1024,512]{1,0:T(8,128)(2,1)S(1)} %copy-done, s32[2048]{0:T(1024)S(1)} %fusion.33), kind=kCustom, calls=%fused_computation.30 | custom fusion | flops 1048576 | bytes 5253124 | tf_op jit(solution)/shard_map/scatter | solution.py:37
  78.4 70.6 %all-to-all-done.1 = bf16[8,4,128,512]{3,2,1,0:T(8,128)(2,1)} async-done(((bf16[8,4,128,512]{3,2,1,0:T(8,128)(2,1)}), bf16[8,4,128,512]{3,2,1,0:T(8,128)(2,1)}, u32[]{:S(2)}, u32[]{:S(2)}) %all-to-all-start.1) | async-done | bytes 4194336 | tf_op jit(solution)/shard_map/all_to_all | solution.py:62
  149.0 4.6 all-to-all-start
  153.6 0.3 all-reduce.3.cloned.1.call-start
  154.6 1.0 broadcast_select_fusion
  155.6 0.0 all-reduce.3.cloned.1.call-update
  155.6 95.5 %all-to-all-done = bf16[8,4,128,512]{3,2,1,0:T(8,128)(2,1)} async-done(((bf16[8,4,128,512]{3,2,1,0:T(8,128)(2,1)}), bf16[8,4,128,512]{3,2,1,0:T(8,128)(2,1)}, u32[]{:S(2)}, u32[]{:S(2)}) %all-to-all-start) | async-done | bytes 4194336 | tf_op jit(solution)/shard_map/all_to_all | solution.py:59
  251.2 7.2 %multiply_reduce_fusion = (f32[8,4,128]{2,0,1:T(8,128)S(1)}, bf16[8,4,128,512]{3,2,0,1:T(8,128)(2,1)S(1)}) fusion(bf16[8,4,128,512]{3,2,1,0:T(8,128)(2,1)} %all-to-all-done.1, f32[4,512,512]{2,1,0:T(8,128)} %param.14, bf16[8,4,128,512]{3,2,1,0:T(8,128)(2,1)} %all-to-all-done), kind=kOutput, calls=%fused_computation.12 | convolution fusion | flops 2159013888 | bytes 16793600 | tf_op jit(solution)/shard_map/srcd,rde->srce/dot_general | solution.py:66
  258.3 2.5 copy.50
  260.8 3.4 copy_convert_fusion
  264.2 4.2 copy.54
  268.4 82.8 %all-reduce.3.cloned.1.call-done = bf16[1024,512]{1,0:T(8,128)(2,1)} async-done(((bf16[1024,512]{1,0:T(8,128)(2,1)}), bf16[1024,512]{1,0:T(8,128)(2,1)}) %all-reduce.3.cloned.1.call-update) | async-done | bytes 1048592 | tf_op jit(solution)/shard_map/psum | solution.py:11
  351.2 0.0 copy-start.4
  351.3 16.5 %fusion = (f32[4096]{0:T(1024)S(1)}, f32[4096,1024]{0,1:T(8,128)}) fusion(bf16[4096,512]{1,0:T(8,128)(2,1)} %bitcast.61, bf16[1024,512]{1,0:T(8,128)(2,1)} %all-reduce.3.cloned.1.call-done), kind=kOutput, calls=%fused_computation.7 | convolution fusion | flops 4324323328 | bytes 22036480 | tf_op jit(solution)/shard_map/dot_general | solution.py:22
  367.8 0.6 copy.52
  368.4 4.4 all-to-all-start.2
  372.8 0.0 copy-done.4
  372.8 0.0 copy-start.1
  372.8 11.3 %fusion.2 = bf16[4096,512]{1,0:T(8,128)(2,1)S(1)} fusion(f32[8,4,128,512]{3,2,1,0:T(8,128)} %copy.54, bf16[1024,512]{1,0:T(8,128)(2,1)S(1)} %copy-done.4, f32[4096,1024]{0,1:T(8,128)} %get-tuple-element.12, f32[4096]{0:T(1024)S(1)} %bitcast.72), kind=kOutput, calls=%fused_computation.11 | convolution fusion | flops 4322230272 | bytes 30425088 | tf_op jit(solution)/shard_map/dot_general | solution.py:26
  384.2 0.0 copy-start.5
  384.2 0.0 copy-done.1
  384.2 2.4 convert_bitcast_fusion
  386.6 0.0 copy-done.5
  386.6 2.2 copy.56
  388.8 0.0 all-to-all-done.2
  388.8 6.0 %all-to-all-start.3 = ((bf16[8,4,128,512]{3,2,1,0:T(8,128)(2,1)}), bf16[8,4,128,512]{3,2,1,0:T(8,128)(2,1)}, u32[]{:S(2)}, u32[]{:S(2)}) async-start(bf16[8,4,128,512]{3,2,1,0:T(8,128)(2,1)} %copy.56), calls=%async_computation.3 | async-start | bytes 8388608 | tf_op jit(solution)/shard_map/all_to_all | solution.py:81
  394.8 0.0 all-reduce.5.cloned.1.call-start
  394.9 7.2 %bitcast_convert_fusion = bf16[4,512,512]{2,1,0:T(8,128)(2,1)} fusion(bf16[8,4,128,512]{3,2,1,0:T(8,128)(2,1)} %all-to-all-done, bf16[8,4,128,512]{3,2,1,0:T(8,128)(2,1)} %bitcast.74), kind=kOutput, calls=%fused_computation.18 | convolution fusion | flops 2148532224 | bytes 10485760 | tf_op jit(solution)/shard_map/srcd,srce->rde/dot_general | solution.py:73
  402.0 0.0 copy-start.3
  402.0 0.0 all-reduce.5.cloned.1.call-update
  402.1 22.1 %gather_fusion = bf16[2048]{0:T(1024)(128)(2,1)} fusion(bf16[4096]{0:T(1024)(128)(2,1)S(1)} %bitcast.58, s32[2048]{0:T(1024)S(1)} %broadcast_clamp_fusion), kind=kCustom, calls=%fused_computation.2 | custom fusion | bytes 16384 | tf_op jit(solution)/shard_map/gather | solution.py:42
  424.2 29.9 %all-reduce.5.cloned.1.call-done = bf16[4,512,512]{2,1,0:T(8,128)(2,1)} async-done(((bf16[4,512,512]{2,1,0:T(8,128)(2,1)}), bf16[4,512,512]{2,1,0:T(8,128)(2,1)}) %all-reduce.5.cloned.1.call-update) | async-done | bytes 2097168 | tf_op jit(solution)/shard_map/psum | solution.py:86
  454.1 2.1 fusion.4
  456.2 0.0 copy-done.3
  456.2 0.6 fusion.39
  456.8 5.5 %fusion.5 = f32[4,512,512]{2,1,0:T(8,128)} fusion(f32[4,512,512]{2,1,0:T(8,128)} %param.14, bf16[4,512,512]{2,1,0:T(8,128)(2,1)} %all-reduce.5.cloned.1.call-done, f32[4,512]{1,0:T(4,128)S(1)} %get-tuple-element.5), kind=kLoop, calls=%fused_computation.17 | loop fusion | flops 3145728 | bytes 10493952 | tf_op jit(solution)/shard_map/sub | solution.py:32
  462.3 23.6 %all-to-all-done.3 = bf16[8,4,128,512]{3,2,1,0:T(8,128)(2,1)} async-done(((bf16[8,4,128,512]{3,2,1,0:T(8,128)(2,1)}), bf16[8,4,128,512]{3,2,1,0:T(8,128)(2,1)}, u32[]{:S(2)}, u32[]{:S(2)}) %all-to-all-start.3) | async-done | bytes 4194336 | tf_op jit(solution)/shard_map/all_to_all | solution.py:81
  485.9 12.0 %gather_fusion.1 = bf16[2048,512]{1,0:T(8,128)(2,1)} fusion(bf16[4096,512]{1,0:T(8,128)(2,1)} %bitcast.21, s32[2048]{0:T(1024)S(1)} %broadcast_clamp_fusion), kind=kCustom, calls=%fused_computation.3 | custom fusion | bytes 4202496 | tf_op jit(solution)/shard_map/gather | solution.py:42
  (6 shorter events, 0.1 us)
Async XLA Ops:
  48.3 7.4 %copy-start.2 = (s32[2048]{0:T(1024)S(1)}, s32[2048]{0:T(1024)}, u32[]{:S(2)}) copy-start(s32[2048]{0:T(1024)} %param.9) | copy-start | bytes 24580
  48.3 7.5 %copy-start = (bf16[1024,512]{1,0:T(8,128)(2,1)S(1)}, bf16[1024,512]{1,0:T(8,128)(2,1)}, u32[]{:S(2)}) copy-start(bf16[1024,512]{1,0:T(8,128)(2,1)} %param.13) | copy-start | bytes 3145732
  48.3 100.7 %all-to-all-start.1 = ((bf16[8,4,128,512]{3,2,1,0:T(8,128)(2,1)}), bf16[8,4,128,512]{3,2,1,0:T(8,128)(2,1)}, u32[]{:S(2)}, u32[]{:S(2)}) async-start(bf16[8,4,128,512]{3,2,1,0:T(8,128)(2,1)} %bitcast.60), calls=%async_computation.1 | async-start | bytes 8388608 | tf_op jit(solution)/shard_map/all_to_all | solution.py:62
  149.0 102.1 %all-to-all-start = ((bf16[8,4,128,512]{3,2,1,0:T(8,128)(2,1)}), bf16[8,4,128,512]{3,2,1,0:T(8,128)(2,1)}, u32[]{:S(2)}, u32[]{:S(2)}) async-start(bf16[8,4,128,512]{3,2,1,0:T(8,128)(2,1)} %bitcast.59), calls=%async_computation | async-start | bytes 8388608 | tf_op jit(solution)/shard_map/all_to_all | solution.py:59
  153.6 197.6 %all-reduce.3.cloned.1.call-start = ((), (), s32[]{:S(2)}) async-start(), calls=%async_computation.4 | async-start | bytes 2097152 | tf_op jit(solution)/shard_map/psum | solution.py:11
  351.2 21.6 %copy-start.4 = (bf16[1024,512]{1,0:T(8,128)(2,1)S(1)}, bf16[1024,512]{1,0:T(8,128)(2,1)}, u32[]{:S(2)}) copy-start(bf16[1024,512]{1,0:T(8,128)(2,1)} %all-reduce.3.cloned.1.call-done) | copy-start | bytes 3145732
  368.4 20.4 %all-to-all-start.2 = ((bf16[8,4,128]{2,1,0:T(4,128)(2,1)}), bf16[8,4,128]{2,1,0:T(4,128)(2,1)S(1)}, u32[]{:S(2)}, u32[]{:S(2)}) async-start(bf16[8,4,128]{2,1,0:T(4,128)(2,1)} %copy.52), calls=%async_computation.2 | async-start | bytes 16384 | tf_op jit(solution)/shard_map/all_to_all | solution.py:82
  372.8 11.3 %copy-start.1 = (f32[4,512,512]{2,1,0:T(8,128)S(1)}, f32[4,512,512]{2,1,0:T(8,128)}, u32[]{:S(2)}) copy-start(f32[4,512,512]{2,1,0:T(8,128)} %param.14) | copy-start | bytes 12582916
  384.2 2.4 copy-start.5
  388.8 97.0 %all-to-all-start.3 = ((bf16[8,4,128,512]{3,2,1,0:T(8,128)(2,1)}), bf16[8,4,128,512]{3,2,1,0:T(8,128)(2,1)}, u32[]{:S(2)}, u32[]{:S(2)}) async-start(bf16[8,4,128,512]{3,2,1,0:T(8,128)(2,1)} %copy.56), calls=%async_computation.3 | async-start | bytes 8388608 | tf_op jit(solution)/shard_map/all_to_all | solution.py:81
  394.8 59.3 %all-reduce.5.cloned.1.call-start = ((), (), s32[]{:S(2)}) async-start(), calls=%async_computation.5 | async-start | bytes 4194304 | tf_op jit(solution)/shard_map/psum | solution.py:86
  402.0 54.1 %copy-start.3 = (f32[4,512]{1,0:T(4,128)S(1)}, f32[4,512]{1,0:T(4,128)}, u32[]{:S(2)}) copy-start(f32[4,512]{1,0:T(4,128)} %param.15) | copy-start | bytes 24580
Sparse Core Ops, SparseCore 0:
  160.2 190.9 all-reduce.2
  402.2 51.8 all-reduce.4
where the time goes:
time: 506 us; the launch traced here: 505 us
  waiting for transfers between devices  303 us (60%)
  other arithmetic  76 us (15%)
  matrix products  44.5 us (9%)
  local copies, waits for them, and re-layouts  44 us (9%)
  starting transfers between devices  22.8 us (5%)
  between operations  14.8 us (3%)
    all_to_all x1, waiting for transfers between devices, per_device(): lax.all_to_all(to_buckets(head_rows, position, layout), 'rel', split_axis...  95.5 us
    psum x1, waiting for transfers between devices, broadcast(): return lax.psum(jnp.where(mine, shard, jnp.zeros_like(shard)), axis)  82.8 us
    all_to_all x1, waiting for transfers between devices, per_device(): lax.all_to_all(to_buckets(tail_rows, position, layout), 'rel', split_axis...  70.6 us
    scatter x2, other arithmetic, to_buckets(): filled = jnp.zeros(flat_shape, values.dtype).at[position].set(values)  50.3 us
    gather x2, local copies, waits for them, and re-layouts, from_buckets(): return stacked.reshape((-1,) + stacked.shape[3:])[position]  34.1 us
    psum x1, waiting for transfers between devices, per_device(): lax.psum(partial_value.astype(jnp.bfloat16), 'grp').astype(jnp.float32)  29.9 us
    all_to_all x1, waiting for transfers between devices, per_device(): lax.all_to_all(head_back, 'rel', split_axis=0, concat_axis=0, tiled=True)  23.6 us
    dot_general x1, matrix products, score_rows(): jnp.dot(query_rows, negatives.T, preferred_element_type=jnp.float32)  16.5 us
  transfers between devices with their start and end apart: 6, of which 5 were waited for; matrix products, arithmetic and copies ran while one was open for 19% of the time, Pallas kernels for 0%

commit v1 on v0

--- a/solution.py
+++ b/solution.py
@@ -77,8 +77,31 @@
         "srce,rde->srcd", grad_rows, matrices, preferred_element_type=jnp.float32
     ).astype(jnp.bfloat16)
     partial_value, head_back = (partial_value, head_back)
+
+    def store_patches_all(base_x, group_axis, on_dim, where_dim=0):
+        side_arr, formed = (lax.axis_size(group_axis), lax.axis_index(group_axis))
+        v_now = list(base_x.shape)
+        all_values = base_x.shape[on_dim] // side_arr
+        v_now[on_dim] = all_values
+        spare = v_now[where_dim]
+        v_now[where_dim] = spare * side_arr
+        u1 = jnp.zeros(v_now, base_x.dtype)
+        for dd in range(side_arr):
+            field_out = lax.dynamic_slice_in_dim(
+                base_x, (formed ^ dd) * all_values, all_values, axis=on_dim
+            )
+            if dd:
+                made = []
+                for idx in range(side_arr):
+                    made.append((idx, idx ^ dd))
+                field_out = lax.ppermute(field_out, axis_name=group_axis, perm=made)
+            u1 = lax.dynamic_update_slice_in_dim(
+                u1, field_out, (formed ^ dd) * spare, axis=where_dim
+            )
+        return u1
+
     back_grads, back_losses = (
-        lax.all_to_all(head_back, "rel", split_axis=0, concat_axis=0, tiled=True),
+        store_patches_all(head_back, "rel", 0),
         lax.all_to_all(slot_losses.reshape(layout), "rel", split_axis=0, concat_axis=0, tiled=True),
     )
     head_grad = from_buckets(back_grads, position)

time: 506 us -> 549 us (1.085)
  the two profiles are of different devices: /device:TPU:0 before, /device:TPU:8 now
where the time goes in v1:
time: 549 us; the launch traced here: 541 us
  waiting for transfers between devices  320 us (58%)
  other arithmetic  76 us (14%)
  local copies, waits for them, and re-layouts  57.5 us (10%)
  matrix products  44.9 us (8%)
  starting transfers between devices  27.5 us (5%)
  between operations  15.1 us (3%)
    psum x1, waiting for transfers between devices, broadcast(): return lax.psum(jnp.where(mine, shard, jnp.zeros_like(shard)), axis)  93.3 us
    all_to_all x1, waiting for transfers between devices, per_device(): lax.all_to_all(to_buckets(tail_rows, position, layout), 'rel', split_axis...  92.5 us
    all_to_all x1, waiting for transfers between devices, per_device(): lax.all_to_all(to_buckets(head_rows, position, layout), 'rel', split_axis...  67.9 us
    scatter x2, other arithmetic, to_buckets(): filled = jnp.zeros(flat_shape, values.dtype).at[position].set(values)  50.3 us
    gather x2, local copies, waits for them, and re-layouts, from_buckets(): return stacked.reshape((-1,) + stacked.shape[3:])[position]  34.1 us
    all_to_all x1, waiting for transfers between devices, per_device(): lax.all_to_all(slot_losses.reshape(layout), 'rel', split_axis=0, concat_a...  33.9 us
    ppermute x7, waiting for transfers between devices, store_patches_all(): field_out = lax.ppermute(field_out, axis_name=group_axis, perm=made)  32.8 us
    dot_general x1, matrix products, score_rows(): jnp.dot(query_rows, negatives.T, preferred_element_type=jnp.float32)  16.2 us
  transfers between devices with their start and end apart: 12, of which 6 were waited for; matrix products, arithmetic and copies ran while one was open for 16% of the time, Pallas kernels for 0%

profile of v1, /device:TPU:8, one launch (start us, length us, event | category | flops | bytes accessed | tf_op | source)
XLA Modules:
  0.0 541.4 jit_solution(917453968259011978)
XLA Ops:
  7.2 0.7 fusion.34
  7.9 0.7 compare_and_fusion.1
  8.6 0.7 fusion.31
  9.3 9.1 %reduce-window.6 = s32[32,16,128]{2,1,0:T(8,128)S(1)} reduce-window(s32[32,16,128]{2,1,0:T(8,128)S(1)} %fusion.31, s32[]{:T(128)} %constant.29.clone.1), window={size=1x1x128 pad=0_0x0_0x127_0}, to_apply=%region_0.0 | reduce-window | flops 8323072 | bytes 524292 | tf_op jit(solution)/shard_map/reduce-window
  18.4 0.1 slice.16
  18.5 0.2 copy.56
  18.7 0.2 reduce-window.9
  18.9 0.1 add_add_fusion
  19.1 0.8 fusion.30
  19.9 0.7 compare_select_fusion.1
  20.6 27.6 %scatter_custom_fusion = bf16[4096,512]{1,0:T(8,128)(2,1)} fusion(s32[2048]{0:T(1024)S(1)} %bitcast.81, bf16[]{:T(256)} %constant.27.clone.1, pred[2048]{0:T(1024)(128)(4,1)S(1)} %compare_and_fusion.1, bf16[]{:T(256)} %constant.15.clone.2, bf16[1024,512]{1,0:T(8,128)(2,1)} %param.13, s32[2048]{0:T(1024)S(1)} %fusion.34), kind=kCustom, calls=%fused_computation.30 | custom fusion | flops 1048576 | bytes 5253124 | tf_op jit(solution)/shard_map/scatter | solution.py:37
  48.2 6.9 %all-to-all-start = ((bf16[8,4,128,512]{3,2,1,0:T(8,128)(2,1)}), bf16[8,4,128,512]{3,2,1,0:T(8,128)(2,1)}, u32[]{:S(2)}, u32[]{:S(2)}) async-start(bf16[8,4,128,512]{3,2,1,0:T(8,128)(2,1)} %bitcast.72), calls=%async_computation | async-start | bytes 8388608 | tf_op jit(solution)/shard_map/all_to_all | solution.py:59
  55.2 0.0 copy-done.3
  55.2 22.7 %scatter_custom_fusion.1 = bf16[4096,512]{1,0:T(8,128)(2,1)} fusion(s32[2048]{0:T(1024)S(1)} %bitcast.82, bf16[]{:T(256)} %constant.27.clone.1, pred[2048]{0:T(1024)(128)(4,1)S(1)} %compare_and_fusion, bf16[]{:T(256)} %constant.15.clone.2, bf16[1024,512]{1,0:T(8,128)(2,1)S(1)} %copy-done, s32[2048]{0:T(1024)S(1)} %fusion.35), kind=kCustom, calls=%fused_computation.28 | custom fusion | flops 1048576 | bytes 5253124 | tf_op jit(solution)/shard_map/scatter | solution.py:37
  77.9 67.9 %all-to-all-done = bf16[8,4,128,512]{3,2,1,0:T(8,128)(2,1)} async-done(((bf16[8,4,128,512]{3,2,1,0:T(8,128)(2,1)}), bf16[8,4,128,512]{3,2,1,0:T(8,128)(2,1)}, u32[]{:S(2)}, u32[]{:S(2)}) %all-to-all-start) | async-done | bytes 4194336 | tf_op jit(solution)/shard_map/all_to_all | solution.py:59
  145.8 7.0 %all-to-all-start.1 = ((bf16[8,4,128,512]{3,2,1,0:T(8,128)(2,1)}), bf16[8,4,128,512]{3,2,1,0:T(8,128)(2,1)}, u32[]{:S(2)}, u32[]{:S(2)}) async-start(bf16[8,4,128,512]{3,2,1,0:T(8,128)(2,1)} %bitcast.71), calls=%async_computation.1 | async-start | bytes 8388608 | tf_op jit(solution)/shard_map/all_to_all | solution.py:62
  153.5 1.0 broadcast_select_fusion
  154.5 0.0 all-reduce.3.cloned.1.call-update
  154.5 0.0 all-reduce.5.cloned.1.call-start
  154.6 92.5 %all-to-all-done.1 = bf16[8,4,128,512]{3,2,1,0:T(8,128)(2,1)} async-done(((bf16[8,4,128,512]{3,2,1,0:T(8,128)(2,1)}), bf16[8,4,128,512]{3,2,1,0:T(8,128)(2,1)}, u32[]{:S(2)}, u32[]{:S(2)}) %all-to-all-start.1) | async-done | bytes 4194336 | tf_op jit(solution)/shard_map/all_to_all | solution.py:62
  247.1 7.1 %multiply_reduce_fusion = (f32[8,4,128]{2,0,1:T(8,128)S(1)}, bf16[8,4,128,512]{3,2,0,1:T(8,128)(2,1)S(1)}) fusion(bf16[8,4,128,512]{3,2,1,0:T(8,128)(2,1)} %all-to-all-done.1, f32[4,512,512]{2,1,0:T(8,128)} %param.14, bf16[8,4,128,512]{3,2,1,0:T(8,128)(2,1)} %all-to-all-done), kind=kOutput, calls=%fused_computation.12 | convolution fusion | flops 2159013888 | bytes 16793600 | tf_op jit(solution)/shard_map/srcd,rde->srce/dot_general | solution.py:66
  254.2 2.5 copy.47
  256.7 93.3 %all-reduce.3.cloned.1.call-done = bf16[1024,512]{1,0:T(8,128)(2,1)} async-done(((bf16[1024,512]{1,0:T(8,128)(2,1)}), bf16[1024,512]{1,0:T(8,128)(2,1)}) %all-reduce.3.cloned.1.call-update) | async-done | bytes 1048592 | tf_op jit(solution)/shard_map/psum | solution.py:11
  350.0 16.2 %fusion = (f32[4096]{0:T(1024)S(1)}, f32[4096,1024]{0,1:T(8,128)}) fusion(bf16[4096,512]{1,0:T(8,128)(2,1)} %bitcast.73, bf16[1024,512]{1,0:T(8,128)(2,1)} %all-reduce.3.cloned.1.call-done), kind=kOutput, calls=%fused_computation.7 | convolution fusion | flops 4324323328 | bytes 22036480 | tf_op jit(solution)/shard_map/dot_general | solution.py:22
  366.3 3.4 copy_convert_fusion
  369.7 1.6 copy.51
  371.3 0.0 copy-start.2
  371.3 11.1 %fusion.2 = bf16[4096,512]{1,0:T(8,128)(2,1)} fusion(f32[8,4,128,512]{3,2,1,0:T(8,128)S(1)} %copy.51, bf16[1024,512]{1,0:T(8,128)(2,1)S(1)} %copy-done.5, f32[4096,1024]{0,1:T(8,128)} %get-tuple-element.19, f32[4096]{0:T(1024)S(1)} %bitcast.84), kind=kOutput, calls=%fused_computation.11 | convolution fusion | flops 4322230272 | bytes 30425088 | tf_op jit(solution)/shard_map/dot_general | solution.py:26
  382.4 4.6 fusion.12
  387.1 1.9 copy-done.1
  389.0 1.0 dynamic-slice_bitcast_fusion
  390.0 1.4 collective-permute-start
  391.4 0.6 collective-permute-start.1
  392.0 5.9 %bitcast_convert_fusion = bf16[4,512,512]{2,1,0:T(8,128)(2,1)} fusion(bf16[8,4,128,512]{3,2,1,0:T(8,128)(2,1)} %all-to-all-done, bf16[8,4,128,512]{3,2,1,0:T(8,128)(2,1)S(1)} %bitcast.86), kind=kOutput, calls=%fused_computation.18 | convolution fusion | flops 2148532224 | bytes 10485760 | tf_op jit(solution)/shard_map/srcd,srce->rde/dot_general | solution.py:73
  397.9 0.0 all-reduce.5.cloned.1.call-update
  397.9 1.6 collective-permute-start.2
  399.5 1.4 collective-permute-start.3
  400.9 2.4 collective-permute-start.4
  403.3 0.6 copy.49
  403.9 4.1 all-to-all-start.2
  408.0 2.5 broadcast_in_dim.14
  410.5 1.9 bitcast_dynamic-update-slice_fusion
  412.4 33.9 %all-to-all-done.2 = bf16[8,4,128]{2,1,0:T(4,128)(2,1)S(1)} async-done(((bf16[8,4,128]{2,1,0:T(4,128)(2,1)}), bf16[8,4,128]{2,1,0:T(4,128)(2,1)S(1)}, u32[]{:S(2)}, u32[]{:S(2)}) %all-to-all-start.2) | async-done | bytes 8224 | tf_op jit(solution)/shard_map/all_to_all | solution.py:105
  446.3 22.1 %gather_fusion = bf16[2048]{0:T(1024)(128)(2,1)} fusion(bf16[4096]{0:T(1024)(128)(2,1)S(1)} %bitcast.70, s32[2048]{0:T(1024)S(1)} %broadcast_clamp_fusion), kind=kCustom, calls=%fused_computation.2 | custom fusion | bytes 16384 | tf_op jit(solution)/shard_map/gather | solution.py:42
  468.3 0.0 collective-permute-done
  468.4 0.5 collective-permute-start.5
  468.9 1.9 constant_dynamic-update-slice_fusion.5
  470.7 0.0 collective-permute-done.1
  470.7 1.5 collective-permute-start.6
  472.2 1.9 constant_dynamic-update-slice_fusion.4
  474.1 0.0 collective-permute-done.2
  474.1 1.9 constant_dynamic-update-slice_fusion.3
  476.0 0.0 collective-permute-done.3
  476.0 1.9 constant_dynamic-update-slice_fusion.2
  477.9 0.0 collective-permute-done.4
  477.9 1.9 constant_dynamic-update-slice_fusion.1
  479.7 24.2 %collective-permute-done.5 = bf16[1,4,128,512]{3,2,1,0:T(8,128)(2,1)S(1)} collective-permute-done((bf16[1,4,128,512]{3,2,1,0:T(8,128)(2,1)S(1)}, bf16[1,4,128,512]{3,2,1,0:T(8,128)(2,1)S(1)}, u32[]{:S(2)}, u32[]{:S(2)}) %collective-permute-start.5) | collective-permute-done | bytes 524320 | tf_op jit(solution)/shard_map/ppermute | solution.py:97
  503.9 0.8 constant_dynamic-update-slice_fusion
  504.8 8.5 %collective-permute-done.6 = bf16[1,4,128,512]{3,2,1,0:T(8,128)(2,1)S(1)} collective-permute-done((bf16[1,4,128,512]{3,2,1,0:T(8,128)(2,1)S(1)}, bf16[1,4,128,512]{3,2,1,0:T(8,128)(2,1)S(1)}, u32[]{:S(2)}, u32[]{:S(2)}) %collective-permute-start.6) | collective-permute-done | bytes 524320 | tf_op jit(solution)/shard_map/ppermute | solution.py:97
  513.3 0.8 constant_dynamic-update-slice_fusion.6
  514.1 12.0 %gather_fusion.1 = bf16[2048,512]{1,0:T(8,128)(2,1)} fusion(bf16[4096,512]{1,0:T(8,128)(2,1)} %bitcast.28, s32[2048]{0:T(1024)S(1)} %broadcast_clamp_fusion), kind=kCustom, calls=%fused_computation.3 | custom fusion | bytes 4202496 | tf_op jit(solution)/shard_map/gather | solution.py:42
  526.1 2.1 fusion.4
  528.2 0.6 fusion.40
  528.8 5.5 %fusion.5 = f32[4,512,512]{2,1,0:T(8,128)} fusion(f32[4,512,512]{2,1,0:T(8,128)} %param.14, bf16[4,512,512]{2,1,0:T(8,128)(2,1)} %all-reduce.5.cloned.1.call-done, f32[4,512]{1,0:T(4,128)S(1)} %get-tuple-element.5), kind=kLoop, calls=%fused_computation.17 | loop fusion | flops 3145728 | bytes 10493952 | tf_op jit(solution)/shard_map/sub | solution.py:32
  (19 shorter events, 0.1 us)
Async XLA Ops:
  48.2 6.9 %copy-start.3 = (s32[2048]{0:T(1024)S(1)}, s32[2048]{0:T(1024)}, u32[]{:S(2)}) copy-start(s32[2048]{0:T(1024)} %param.11) | copy-start | bytes 24580
  48.2 7.0 %copy-start = (bf16[1024,512]{1,0:T(8,128)(2,1)S(1)}, bf16[1024,512]{1,0:T(8,128)(2,1)}, u32[]{:S(2)}) copy-start(bf16[1024,512]{1,0:T(8,128)(2,1)} %param.13) | copy-start | bytes 3145732
  48.2 97.6 %all-to-all-start = ((bf16[8,4,128,512]{3,2,1,0:T(8,128)(2,1)}), bf16[8,4,128,512]{3,2,1,0:T(8,128)(2,1)}, u32[]{:S(2)}, u32[]{:S(2)}) async-start(bf16[8,4,128,512]{3,2,1,0:T(8,128)(2,1)} %bitcast.72), calls=%async_computation | async-start | bytes 8388608 | tf_op jit(solution)/shard_map/all_to_all | solution.py:59
  145.8 101.3 %all-to-all-start.1 = ((bf16[8,4,128,512]{3,2,1,0:T(8,128)(2,1)}), bf16[8,4,128,512]{3,2,1,0:T(8,128)(2,1)}, u32[]{:S(2)}, u32[]{:S(2)}) async-start(bf16[8,4,128,512]{3,2,1,0:T(8,128)(2,1)} %bitcast.71), calls=%async_computation.1 | async-start | bytes 8388608 | tf_op jit(solution)/shard_map/all_to_all | solution.py:62
  152.8 197.2 %all-reduce.3.cloned.1.call-start = ((), (), s32[]{:S(2)}) async-start(), calls=%async_computation.3 | async-start | bytes 2097152 | tf_op jit(solution)/shard_map/psum | solution.py:11
  154.5 371.6 %all-reduce.5.cloned.1.call-start = ((), (), s32[]{:S(2)}) async-start(), calls=%async_computation.4 | async-start | bytes 4194304 | tf_op jit(solution)/shard_map/psum | solution.py:109
  369.7 1.6 copy-start.5
  371.3 11.1 %copy-start.2 = (f32[4,512,512]{2,1,0:T(8,128)S(1)}, f32[4,512,512]{2,1,0:T(8,128)}, u32[]{:S(2)}) copy-start(f32[4,512,512]{2,1,0:T(8,128)} %param.14) | copy-start | bytes 12582916
  387.0 1.9 copy-start.1
  389.0 3.0 copy-start.6
  390.0 78.3 %collective-permute-start = (bf16[1,4,128,512]{3,2,1,0:T(8,128)(2,1)}, bf16[1,4,128,512]{3,2,1,0:T(8,128)(2,1)}, u32[]{:S(2)}, u32[]{:S(2)}) collective-permute-start(bf16[1,4,128,512]{3,2,1,0:T(8,128)(2,1)} %get-tuple-element.13), channel_id=1, source_target_pairs={{0,1},{1,0},{2,3},{3,2},{4,5},{5,4},{6,7},{7,6},{8,9},{9,8},{10,11... | collective-permute-start | bytes 1572872 | tf_op jit(solution)/shard_map/ppermute | solution.py:97
  391.4 79.3 %collective-permute-start.1 = (bf16[1,4,128,512]{3,2,1,0:T(8,128)(2,1)S(1)}, bf16[1,4,128,512]{3,2,1,0:T(8,128)(2,1)}, u32[]{:S(2)}, u32[]{:S(2)}) collective-permute-start(bf16[1,4,128,512]{3,2,1,0:T(8,128)(2,1)S(1)} %get-tuple-element.12), channel_id=1, source_target_pairs={{0,2},{1,3},{2,0},{3,1},{4,6},{5,7},{6,4},{7,5},{8,10},{9,11},{10,... | collective-permute-start | bytes 1572872 | tf_op jit(solution)/shard_map/ppermute | solution.py:97
  397.9 76.2 %collective-permute-start.2 = (bf16[1,4,128,512]{3,2,1,0:T(8,128)(2,1)S(1)}, bf16[1,4,128,512]{3,2,1,0:T(8,128)(2,1)}, u32[]{:S(2)}, u32[]{:S(2)}) collective-permute-start(bf16[1,4,128,512]{3,2,1,0:T(8,128)(2,1)S(1)} %get-tuple-element.11), channel_id=1, source_target_pairs={{0,3},{1,2},{2,1},{3,0},{4,7},{5,6},{6,5},{7,4},{8,11},{9,10},{10,... | collective-permute-start | bytes 1572872 | tf_op jit(solution)/shard_map/ppermute | solution.py:97
  399.5 76.5 %collective-permute-start.3 = (bf16[1,4,128,512]{3,2,1,0:T(8,128)(2,1)S(1)}, bf16[1,4,128,512]{3,2,1,0:T(8,128)(2,1)}, u32[]{:S(2)}, u32[]{:S(2)}) collective-permute-start(bf16[1,4,128,512]{3,2,1,0:T(8,128)(2,1)S(1)} %get-tuple-element.10), channel_id=1, source_target_pairs={{0,4},{1,5},{2,6},{3,7},{4,0},{5,1},{6,2},{7,3},{8,12},{9,13},{10,... | collective-permute-start | bytes 1572872 | tf_op jit(solution)/shard_map/ppermute | solution.py:97
  400.9 77.0 %collective-permute-start.4 = (bf16[1,4,128,512]{3,2,1,0:T(8,128)(2,1)S(1)}, bf16[1,4,128,512]{3,2,1,0:T(8,128)(2,1)}, u32[]{:S(2)}, u32[]{:S(2)}) collective-permute-start(bf16[1,4,128,512]{3,2,1,0:T(8,128)(2,1)S(1)} %get-tuple-element.9), channel_id=1, source_target_pairs={{0,5},{1,4},{2,7},{3,6},{4,1},{5,0},{6,3},{7,2},{8,13},{9,12},{10,... | collective-permute-start | bytes 1572872 | tf_op jit(solution)/shard_map/ppermute | solution.py:97
  403.9 42.4 %all-to-all-start.2 = ((bf16[8,4,128]{2,1,0:T(4,128)(2,1)}), bf16[8,4,128]{2,1,0:T(4,128)(2,1)S(1)}, u32[]{:S(2)}, u32[]{:S(2)}) async-start(bf16[8,4,128]{2,1,0:T(4,128)(2,1)} %copy.49), calls=%async_computation.2 | async-start | bytes 16384 | tf_op jit(solution)/shard_map/all_to_all | solution.py:105
  468.4 35.6 %collective-permute-start.5 = (bf16[1,4,128,512]{3,2,1,0:T(8,128)(2,1)S(1)}, bf16[1,4,128,512]{3,2,1,0:T(8,128)(2,1)S(1)}, u32[]{:S(2)}, u32[]{:S(2)}) collective-permute-start(bf16[1,4,128,512]{3,2,1,0:T(8,128)(2,1)S(1)} %get-tuple-element.8), channel_id=1, source_target_pairs={{0,6},{1,7},{2,4},{3,5},{4,2},{5,3},{6,0},{7,1},{8,14},{9,15},{10,... | collective-permute-start | bytes 1572872 | tf_op jit(solution)/shard_map/ppermute | solution.py:97
  470.7 42.5 %collective-permute-start.6 = (bf16[1,4,128,512]{3,2,1,0:T(8,128)(2,1)S(1)}, bf16[1,4,128,512]{3,2,1,0:T(8,128)(2,1)S(1)}, u32[]{:S(2)}, u32[]{:S(2)}) collective-permute-start(bf16[1,4,128,512]{3,2,1,0:T(8,128)(2,1)S(1)} %get-tuple-element.7), channel_id=1, source_target_pairs={{0,7},{1,6},{2,5},{3,4},{4,3},{5,2},{6,1},{7,0},{8,15},{9,14},{10,... | collective-permute-start | bytes 1572872 | tf_op jit(solution)/shard_map/ppermute | solution.py:97
  514.1 14.1 %copy-start.4 = (f32[4,512]{1,0:T(4,128)S(1)}, f32[4,512]{1,0:T(4,128)}, u32[]{:S(2)}) copy-start(f32[4,512]{1,0:T(4,128)} %param.15) | copy-start | bytes 24580
Sparse Core Ops, SparseCore 0:
  159.4 190.6 all-reduce.2
  398.1 50.3 all-reduce.4
